TPU v7x, 512 devices: a whole 4x8x8 slice. The times are simulated.
512 devices in a mesh: rep: 32 (over x, z), tp: 16 (over y, core).
Axes of the slice: x: 4, y: 8, z: 8, core: 2. Of those that a mesh axis runs over, the one named last changes fastest.
Arguments:
- queries: bfloat16 [10240, 8192], P('rep', 'tp'), may hold values from -30 to 30
- fresh_kv: bfloat16 [10240, 4096], P('rep', 'tp'), may hold values from -6 to 6, as said below
- kv_cache: bfloat16 [1408, 16, 8, 256], P('rep', 'tp'), may hold values from -6 to 6, as said below
- cached_len: int32 [640], P('rep'), may hold values from 1 to 48, as said below
- page_table: int32 [640, 6], P('rep'), may hold values from 0 to 43, as said below
- out_weight: bfloat16 [8192, 4096], P('tp'), may hold values from -0.09375 to 0.09375
- adapter_down: bfloat16 [64, 64, 8192], P('rep', None, 'tp'), may hold values from -0.0625 to 0.0625
- pooled_up_weight: bfloat16 [64, 64, 4096], P('rep', None, 'tp'), may hold values from -0.75 to 0.75
- adapter_ids: int32 [640], P('rep'), may hold values from 0 to 63, as said below
- pool_slot: int32 [64], replicated, may hold values from 0 to 63, as said below
Outputs:
- adapted_output: bfloat16 [10240, 4096], P('rep', 'tp')
Inputs may be any that keep to these rules, and one draw needn't show every extreme that they name: `kv_cache`: slots that hold the same key-value head are equal. `fresh_kv`: slots that hold the same key-value head are equal. `cached_len`: A row with cached length n uses its first ceil(n / 8) page table entries; in every replica some row has 48. `page_table`: entries index the 44 pages of the row's own replica. The pages that a row uses are distinct, no page is used by two rows of one replica, every page of a replica is used, and entries past a row's used pages repeat its first page. `adapter_ids`: row r of replica i is entry i * 20 + r. The owner of adapter a is replica pool_slot[a] // 2. Within one replica at most 2 rows name adapters of one owner, and one owner, the same for all replicas, is named by exactly 2 rows of every replica. A permutation: adapter a's blocks are adapter_down[pool_slot[a]] and pooled_up_weight[pool_slot[a]].
All inputs are finite; a program needn't handle non-finite values.
Results may differ from a plain program's by a relative error of at most 0.023.
Values may be sent and summed in bfloat16 or wider, within the bound.
No kernel may reach another device: no remote copies, remote signals or barrier semaphores. Data moves between devices by JAX's collectives and lax.ppermute only.
A program may use at most 64 MiB of HBM per device.

v0:
```python
import math
import jax
import jax.numpy as jnp
from jax import lax
from jax.sharding import PartitionSpec as P

ADAPTER_SCALE = 2.0


def shards(
    queries,
    fresh_kv,
    kv_cache,
    cached_len,
    page_table,
    out_weight,
    adapter_down,
    pooled_up_weight,
    adapter_ids,
    pool_slot,
):
    row_count = cached_len.shape[0]
    token_count = queries.shape[0]
    per_row = token_count // row_count
    slot_count = kv_cache.shape[1]
    page_len = kv_cache.shape[2]
    head_dim = kv_cache.shape[3] // 2
    feat_width = queries.shape[1]
    head_count = feat_width // head_dim
    heads_per_slot = head_count // slot_count
    cache_span = page_table.shape[1] * page_len
    output_columns = pooled_up_weight.shape[2]
    paged_kv = (
        kv_cache[page_table]
        .transpose(0, 2, 1, 3, 4)
        .reshape(row_count, slot_count, cache_span, 2 * head_dim)
    )
    recent = fresh_kv.reshape(row_count, per_row, slot_count, 2 * head_dim).transpose(0, 2, 1, 3)
    entries = jnp.concatenate([paged_kv, recent], axis=2)
    key_part = entries[..., :head_dim]
    value_part = entries[..., head_dim:]
    query_rows = queries.reshape(
        row_count, per_row, slot_count, heads_per_slot, head_dim
    ).transpose(0, 2, 1, 3, 4)
    query_rows = query_rows.reshape(row_count, slot_count, per_row * heads_per_slot, head_dim)
    scores = jnp.einsum(
        "rsad,rskd->rsak", query_rows, key_part, preferred_element_type=jnp.float32
    ) / math.sqrt(head_dim)
    entry_ids = jnp.arange(cache_span + per_row)[None, None, None, :]
    token_ids = (jnp.arange(per_row * heads_per_slot) // heads_per_slot)[None, None, :, None]
    allowed = jnp.where(
        entry_ids < cache_span,
        entry_ids < cached_len[:, None, None, None],
        entry_ids - cache_span <= token_ids,
    )
    scores = jnp.where(allowed, scores, -jnp.inf)
    peak_score = jnp.max(scores, axis=-1, keepdims=True)
    raised = jnp.exp(scores - peak_score)
    weights = (raised / jnp.sum(raised, axis=-1, keepdims=True)).astype(jnp.bfloat16)
    attended = jnp.einsum(
        "rsak,rskd->rsad", weights, value_part, preferred_element_type=jnp.float32
    ).astype(jnp.bfloat16)
    attended = attended.reshape(row_count, slot_count, per_row, heads_per_slot, head_dim).transpose(
        0, 2, 1, 3, 4
    )
    attended = attended.reshape(token_count, feat_width)
    plain_output = (
        lax.psum_scatter(
            lax.dot_general(
                out_weight, attended, (((0,), (1,)), ((), ())), preferred_element_type=jnp.float32
            ).astype(jnp.bfloat16),
            "tp",
            scatter_dimension=0,
            tiled=True,
        )
        .astype(jnp.float32)
        .T
    )
    slot_hits = adapter_ids[:, None] == jnp.arange(pool_slot.shape[0])[None, :]
    pool_position = jnp.sum(jnp.where(slot_hits, pool_slot[None, :], 0), axis=1)
    replicas = lax.axis_size("rep")
    local_count = adapter_down.shape[0]
    capacity = (row_count + replicas - 1) // replicas + 1
    owner_of = pool_position // local_count
    local_slot = pool_position % local_count
    same_owner = owner_of[:, None] == owner_of[None, :]
    earlier = jnp.arange(row_count)[None, :] < jnp.arange(row_count)[:, None]
    seat_of = jnp.sum(same_owner & earlier, axis=1)
    target = owner_of * capacity + seat_of
    placing = jnp.arange(replicas * capacity)[:, None] == target[None, :]
    placing_mat = placing.astype(jnp.bfloat16)
    by_row = attended.reshape(row_count, per_row, feat_width)
    send_rows = jnp.einsum(
        "sr,rqf->sqf", placing_mat, by_row, preferred_element_type=jnp.float32
    ).astype(jnp.bfloat16)
    seat_slot = jnp.sum(jnp.where(placing, local_slot[None, :], 0), axis=1).astype(jnp.bfloat16)
    marker = jnp.broadcast_to(seat_slot[:, None, None], (replicas * capacity, 1, feat_width))
    payload = jnp.concatenate([send_rows, marker], axis=1).reshape(
        replicas, capacity, per_row + 1, feat_width
    )
    arrived = lax.all_to_all(payload, "rep", split_axis=0, concat_axis=0, tiled=True)
    arrived = arrived.reshape(replicas * capacity, per_row + 1, feat_width)
    seat_rows = arrived[:, :per_row, :]
    wants_one = arrived[:, per_row, 0] > 0.5
    shrink_both = jnp.einsum(
        "sqf,jkf->jsqk", seat_rows, adapter_down, preferred_element_type=jnp.float32
    )
    shrink_part = jnp.where(wants_one[:, None, None], shrink_both[1], shrink_both[0])
    down_projected = lax.psum(shrink_part.astype(jnp.bfloat16), "tp")
    up_both = jnp.einsum(
        "sqk,jkd->jsqd", down_projected, pooled_up_weight, preferred_element_type=jnp.float32
    )
    seat_delta = jnp.where(wants_one[:, None, None], up_both[1], up_both[0]).astype(jnp.bfloat16)
    returned = lax.all_to_all(
        seat_delta.reshape(replicas, capacity, per_row, output_columns),
        "rep",
        split_axis=0,
        concat_axis=0,
        tiled=True,
    ).reshape(replicas * capacity, per_row, output_columns)
    adapter_correction = jnp.einsum(
        "sr,sqd->rqd", placing_mat, returned, preferred_element_type=jnp.float32
    )
    adapted_output = plain_output + ADAPTER_SCALE * adapter_correction.reshape(
        token_count, output_columns
    )
    return adapted_output.astype(jnp.bfloat16)


def solution(mesh):
    return jax.shard_map(
        shards,
        mesh=mesh,
        in_specs=(
            P("rep", "tp"),
            P("rep", "tp"),
            P("rep", "tp", None, None),
            P("rep"),
            P("rep", None),
            P("tp", None),
            P("rep", None, "tp"),
            P("rep", None, "tp"),
            P("rep"),
            P(),
        ),
        out_specs=P("rep", "tp"),
        check_vma=False,
    )
```

profile of v0, /device:TPU:25, one launch (start us, length us, event | category | flops | bytes accessed | tf_op | source)
XLA Modules:
  0.0 249.2 jit_solution(3435918056866313754)
XLA Ops:
  6.5 0.0 copy-start
  6.5 0.8 iota_compare_fusion.3
  7.3 0.7 compare_select_fusion
  8.0 0.1 copy.33
  8.1 0.1 reshape.203
  8.2 1.2 reshape.194
  9.4 0.1 broadcast_compare_fusion
  9.5 0.0 copy-done
  9.5 0.7 gather_fusion
  10.2 0.4 fusion.37
  10.6 0.0 copy-start.4
  10.6 0.0 copy-start.5
  10.6 0.3 fusion.5
  10.9 0.3 copy-done.4
  11.3 0.0 copy-done.5
  11.3 0.2 select_reduce_fusion.1
  11.5 0.2 convert_reduce_fusion
  11.7 0.1 select_reduce_fusion
  11.8 0.3 convolution_convert_fusion.2
  12.1 0.2 reshape_reshape_transpose_reshape.3
  12.3 0.6 convolution_convert_fusion.1
  12.9 0.1 broadcast_in_dim.107
  13.0 0.1 pad_maximum_fusion
  13.1 0.5 reshape.196
  13.5 1.8 copy.36
  15.3 12.9 %all-to-all-start = ((bf16[32,2,17,512]{3,1,2,0:T(2,128)(2,1)}), bf16[32,2,17,512]{3,1,2,0:T(2,128)(2,1)S(1)}, u32[]{:S(2)}, u32[]{:S(2)}) async-start(bf16[32,2,17,512]{3,1,2,0:T(2,128)(2,1)} %copy.36), calls=%async_computation.1 | async-start | bytes 2228224 | tf_op jit(solution)/shard_map/all_to_all | solution.py:101
  28.2 0.0 copy-start.3
  28.2 0.0 all-reduce.2.cloned.1.call-start
  28.2 0.2 reshape_transpose_reshape.4
  28.5 26.2 %all-to-all-done = bf16[32,2,17,512]{3,1,2,0:T(2,128)(2,1)S(1)} async-done(((bf16[32,2,17,512]{3,1,2,0:T(2,128)(2,1)}), bf16[32,2,17,512]{3,1,2,0:T(2,128)(2,1)S(1)}, u32[]{:S(2)}, u32[]{:S(2)}) %all-to-all-start) | async-done | bytes 1114144 | tf_op jit(solution)/shard_map/all_to_all | solution.py:101
  54.7 0.3 copy.37
  55.0 1.2 compare_reduce_fusion
  56.2 0.4 convolution_bitcast_fusion.1
  56.7 0.9 fusion.7
  57.5 0.0 all-reduce.2.cloned.1.call-update
  57.6 0.0 reduce-scatter.2.cloned.1.call-start
  57.6 5.2 %fusion.1 = bf16[4096,320]{0,1:T(8,128)(2,1)} fusion(bf16[320,512]{1,0:T(8,128)(2,1)S(1)} %reshape_transpose_reshape.4, bf16[512,4096]{1,0:T(8,128)(2,1)} %param.15), kind=kOutput, calls=%fused_computation.3 | convolution fusion | flops 1343488000 | bytes 7143424 | tf_op jit(solution)/shard_map/dot_general | solution.py:69
  62.8 0.0 reduce-scatter.2.cloned.1.call-update
  62.9 0.1 broadcast_in_dim.108
  63.0 110.7 %all-reduce.2.cloned.1.call-done = bf16[64,16,64]{2,1,0:T(8,128)(2,1)} async-done(((bf16[64,16,64]{2,1,0:T(8,128)(2,1)}), bf16[64,16,64]{2,1,0:T(8,128)(2,1)}) %all-reduce.2.cloned.1.call-update) | async-done | bytes 131088 | tf_op jit(solution)/shard_map/psum | solution.py:109
  173.7 1.4 convolution_bitcast_fusion
  175.0 0.1 fusion.36
  175.1 0.1 select_convert_fusion
  175.3 26.2 %all_to_all.10 = bf16[32,2,16,256]{3,2,1,0:T(8,128)(2,1)S(1)} all-to-all(bf16[32,2,16,256]{3,2,1,0:T(8,128)(2,1)S(1)} %select_convert_fusion), channel_id=1, replica_groups=mesh['rep'=32,'tp'=16] {'rep'}, dimensions={0} | all-to-all | bytes 1048576 | tf_op jit(solution)/shard_map/all_to_all | solution.py:114
  201.4 0.3 convolution_multiply_fusion.1
  201.7 0.1 copy.40
  201.8 38.9 %reduce-scatter.2.cloned.1.call-done = bf16[256,320]{0,1:T(8,128)(2,1)} async-done(((bf16[4096,320]{0,1:T(8,128)(2,1)}), bf16[256,320]{0,1:T(8,128)(2,1)}) %reduce-scatter.2.cloned.1.call-update) | async-done | bytes 163856 | tf_op jit(solution)/shard_map/reduce_scatter | solution.py:68
  240.7 1.6 fusion.16
  (11 shorter events, 0.1 us)
Async XLA Ops:
  6.5 2.9 %copy-start = (bf16[44,1,8,256]{3,2,1,0:T(8,128)(2,1)S(1)}, bf16[44,1,8,256]{3,2,1,0:T(8,128)(2,1)}, u32[]{:S(2)}) copy-start(bf16[44,1,8,256]{3,2,1,0:T(8,128)(2,1)} %param.12) | copy-start | bytes 540676
  6.5 3.6 %copy-start.2 = (bf16[320,256]{1,0:T(8,128)(2,1)S(1)}, bf16[320,256]{1,0:T(8,128)(2,1)}, u32[]{:S(2)}) copy-start(bf16[320,256]{1,0:T(8,128)(2,1)} %param.11) | copy-start | bytes 491524
  10.6 0.7 copy-start.4
  10.6 0.7 copy-start.5
  15.3 39.4 %all-to-all-start = ((bf16[32,2,17,512]{3,1,2,0:T(2,128)(2,1)}), bf16[32,2,17,512]{3,1,2,0:T(2,128)(2,1)S(1)}, u32[]{:S(2)}, u32[]{:S(2)}) async-start(bf16[32,2,17,512]{3,1,2,0:T(2,128)(2,1)} %copy.36), calls=%async_computation.1 | async-start | bytes 2228224 | tf_op jit(solution)/shard_map/all_to_all | solution.py:101
  28.2 28.0 %copy-start.3 = (bf16[2,64,512]{2,1,0:T(8,128)(2,1)S(1)}, bf16[2,64,512]{2,1,0:T(8,128)(2,1)}, u32[]{:S(2)}) copy-start(bf16[2,64,512]{2,1,0:T(8,128)(2,1)} %param.16) | copy-start | bytes 393220
  28.2 145.5 %all-reduce.2.cloned.1.call-start = ((), (), s32[]{:S(2)}) async-start(), calls=%async_computation.4 | async-start | bytes 524288 | tf_op jit(solution)/shard_map/psum | solution.py:109
  57.6 183.1 %reduce-scatter.2.cloned.1.call-start = ((), (), s32[]{:S(2)}) async-start(), calls=%async_computation.3 | async-start | bytes 2785280 | tf_op jit(solution)/shard_map/reduce_scatter | solution.py:68
  62.8 110.8 %copy-start.1 = (bf16[2,64,256]{2,1,0:T(8,128)(2,1)S(1)}, bf16[2,64,256]{2,1,0:T(8,128)(2,1)}, u32[]{:S(2)}) copy-start(bf16[2,64,256]{2,1,0:T(8,128)(2,1)} %param.17) | copy-start | bytes 196612
Sparse Core Ops, SparseCore 0:
  57.7 115.9 all-reduce.1
  176.5 64.1 reduce-scatter.1
where the time goes:
time: 250 us; the launch traced here: 249 us
  waiting for transfers between devices  176 us (70%)
  blocking collectives  26.2 us (10%)
  between operations  13.6 us (5%)
  starting transfers between devices  13 us (5%)
  matrix products  8.95 us (4%)
  other arithmetic  5.98 us (2%)
  local copies, waits for them, and re-layouts  5.7 us (2%)
    psum x1, waiting for transfers between devices, shards(): down_projected = lax.psum(shrink_part.astype(jnp.bfloat16), 'tp')  111 us
    reduce_scatter x1, waiting for transfers between devices, shards(): lax.psum_scatter(lax.dot_general(out_weight, attended, (((0,), (1,)), (()...  38.9 us
    all_to_all x1, waiting for transfers between devices, shards(): lax.all_to_all(payload, 'rep', split_axis=0, concat_axis=0, tiled=True)  26.2 us
    all_to_all x1, blocking collectives, shards(): lax.all_to_all(seat_delta.reshape(replicas, capacity, per_row, output_col...  26.2 us
    all_to_all x1, starting transfers between devices, shards(): lax.all_to_all(payload, 'rep', split_axis=0, concat_axis=0, tiled=True)  12.9 us
    dot_general x1, matrix products, shards(): lax.dot_general(out_weight, attended, (((0,), (1,)), ((), ())), preferred...  5.22 us
  transfers between devices with their start and end apart: 3, of which 3 were waited for; matrix products, arithmetic and copies ran while one was open for 3% of the time, Pallas kernels for 0%

commit v1 on v0

--- a/solution.py
+++ b/solution.py
@@ -106,7 +106,8 @@
         "sqf,jkf->jsqk", seat_rows, adapter_down, preferred_element_type=jnp.float32
     )
     shrink_part = jnp.where(wants_one[:, None, None], shrink_both[1], shrink_both[0])
-    down_projected = lax.psum(shrink_part.astype(jnp.bfloat16), "tp")
+    press_the_roads = lambda row_data, comm_axis: jnp.sum(lax.all_gather(row_data, comm_axis), 0)
+    down_projected = press_the_roads(shrink_part.astype(jnp.bfloat16), "tp")
     up_both = jnp.einsum(
         "sqk,jkd->jsqd", down_projected, pooled_up_weight, preferred_element_type=jnp.float32
     )

time: 250 us -> 183 us (0.73)
  the two profiles are of different devices: /device:TPU:25 before, /device:TPU:27 now
where the time goes in v1:
time: 183 us; the launch traced here: 182 us
  waiting for transfers between devices  80.6 us (44%)
  blocking collectives  66.1 us (36%)
  between operations  13.6 us (7%)
  other arithmetic  9.19 us (5%)
  matrix products  8.04 us (4%)
  local copies, waits for them, and re-layouts  4.7 us (3%)
    all_to_all x1, blocking collectives, shards(): lax.all_to_all(payload, 'rep', split_axis=0, concat_axis=0, tiled=True)  42.4 us
    all_gather x1, waiting for transfers between devices, shards(): lax.all_gather(row_data, comm_axis)  42 us
    reduce_scatter x1, waiting for transfers between devices, shards(): lax.psum_scatter(lax.dot_general(out_weight, attended, (((0,), (1,)), (()...  38.5 us
    all_to_all x1, blocking collectives, shards(): lax.all_to_all(seat_delta.reshape(replicas, capacity, per_row, output_col...  23.7 us
    dot_general x1, matrix products, shards(): lax.dot_general(out_weight, attended, (((0,), (1,)), ((), ())), preferred...  5.25 us
  transfers between devices with their start and end apart: 2, of which 2 were waited for; matrix products, arithmetic and copies ran while one was open for 5% of the time, Pallas kernels for 0%

profile of v1, /device:TPU:27, one launch (start us, length us, event | category | flops | bytes accessed | tf_op | source)
XLA Modules:
  0.0 182.2 jit_solution(8570929437844157034)
XLA Ops:
  6.5 0.0 copy-start
  6.6 0.8 iota_compare_fusion.3
  7.3 0.7 compare_select_fusion
  8.0 0.1 copy.30
  8.1 0.1 reshape.203
  8.2 1.2 reshape.194
  9.4 0.1 broadcast_compare_fusion
  9.5 0.0 copy-done
  9.5 0.7 gather_fusion
  10.2 0.0 copy-done.2
  10.2 0.4 fusion.36
  10.6 0.0 copy-start.4
  10.6 0.0 copy-start.5
  10.6 0.3 fusion.5
  11.0 0.3 copy-done.4
  11.3 0.0 copy-done.5
  11.3 0.2 select_reduce_fusion.1
  11.5 0.2 convert_reduce_fusion
  11.7 0.1 select_reduce_fusion
  11.8 0.3 convolution_convert_fusion.2
  12.1 0.2 reshape_reshape_transpose_reshape.3
  12.3 0.6 convolution_convert_fusion.1
  12.9 0.1 broadcast_in_dim.107
  13.0 0.1 pad_maximum_fusion
  13.1 0.5 reshape.196
  13.6 0.8 copy.33
  14.3 42.4 %all_to_all.10 = bf16[32,2,17,512]{3,1,2,0:T(2,128)(2,1)S(1)} all-to-all(bf16[32,2,17,512]{3,1,2,0:T(2,128)(2,1)S(1)} %copy.33), channel_id=1, replica_groups=mesh['rep'=32,'tp'=16] {'rep'}, dimensions={0} | all-to-all | bytes 2228224 | tf_op jit(solution)/shard_map/all_to_all | solution.py:101
  56.7 0.3 copy.34
  57.0 1.2 compare_reduce_fusion
  58.3 0.5 convolution_bitcast_fusion.1
  58.7 0.9 fusion.6
  59.6 0.0 all-gather.2.cloned.1.call-update
  59.6 0.0 reduce-scatter.2.cloned.1.call-start
  59.7 0.2 reshape_transpose_reshape.4
  59.9 5.2 %fusion.1 = bf16[4096,320]{0,1:T(8,128)(2,1)} fusion(bf16[320,512]{1,0:T(8,128)(2,1)S(1)} %reshape_transpose_reshape.4, bf16[512,4096]{1,0:T(8,128)(2,1)} %param.15), kind=kOutput, calls=%fused_computation.3 | convolution fusion | flops 1343488000 | bytes 7143424 | tf_op jit(solution)/shard_map/dot_general | solution.py:69
  65.1 0.0 reduce-scatter.2.cloned.1.call-update
  65.1 0.1 broadcast_in_dim.108
  65.3 0.0 copy-start.1
  65.3 42.0 %all-gather.2.cloned.1.call-done = bf16[16,64,16,64]{3,2,0,1:T(8,128)(2,1)} async-done(((bf16[1,64,16,64]{3,2,0,1:T(8,128)(2,1)}), bf16[16,64,16,64]{3,2,0,1:T(8,128)(2,1)}) %all-gather.2.cloned.1.call-update) | async-done | bytes 2097168 | tf_op jit(solution)/shard_map/all_gather | solution.py:109
  107.3 3.2 %reduce_sum.52 = bf16[64,16,64]{2,1,0:T(8,128)(2,1)S(1)} reduce(bf16[16,64,16,64]{3,2,0,1:T(8,128)(2,1)} %all-gather.2.cloned.1.call-done, bf16[]{:T(256)} %constant.60.clone.1), dimensions={0}, to_apply=%region_6.7 | reduce | flops 983040 | bytes 2228226 | tf_op jit(solution)/shard_map/reduce_sum | solution.py:109
  110.5 0.4 convolution_bitcast_fusion
  110.9 0.1 fusion.35
  111.0 0.1 select_convert_fusion
  111.1 23.7 %all_to_all.11 = bf16[32,2,16,256]{3,2,1,0:T(8,128)(2,1)S(1)} all-to-all(bf16[32,2,16,256]{3,2,1,0:T(8,128)(2,1)S(1)} %select_convert_fusion), channel_id=1, replica_groups=mesh['rep'=32,'tp'=16] {'rep'}, dimensions={0} | all-to-all | bytes 1048576 | tf_op jit(solution)/shard_map/all_to_all | solution.py:115
  134.8 0.3 convolution_multiply_fusion.1
  135.1 0.1 copy.36
  135.2 38.5 %reduce-scatter.2.cloned.1.call-done = bf16[256,320]{0,1:T(8,128)(2,1)} async-done(((bf16[4096,320]{0,1:T(8,128)(2,1)}), bf16[256,320]{0,1:T(8,128)(2,1)}) %reduce-scatter.2.cloned.1.call-update) | async-done | bytes 163856 | tf_op jit(solution)/shard_map/reduce_scatter | solution.py:68
  173.8 1.6 fusion.15
  (11 shorter events, 0.1 us)
Async XLA Ops:
  6.5 3.0 %copy-start = (bf16[44,1,8,256]{3,2,1,0:T(8,128)(2,1)S(1)}, bf16[44,1,8,256]{3,2,1,0:T(8,128)(2,1)}, u32[]{:S(2)}) copy-start(bf16[44,1,8,256]{3,2,1,0:T(8,128)(2,1)} %param.12) | copy-start | bytes 540676
  6.5 3.6 %copy-start.2 = (bf16[320,256]{1,0:T(8,128)(2,1)S(1)}, bf16[320,256]{1,0:T(8,128)(2,1)}, u32[]{:S(2)}) copy-start(bf16[320,256]{1,0:T(8,128)(2,1)} %param.11) | copy-start | bytes 491524
  6.5 100.7 %all-gather.2.cloned.1.call-start = ((), (), s32[]{:S(2)}) async-start(), calls=%async_computation.4 | async-start | bytes 4456448 | tf_op jit(solution)/shard_map/all_gather | solution.py:109
  10.6 0.7 copy-start.4
  10.6 0.7 copy-start.5
  56.7 1.6 copy-start.3
  59.6 114.2 %reduce-scatter.2.cloned.1.call-start = ((), (), s32[]{:S(2)}) async-start(), calls=%async_computation.3 | async-start | bytes 2785280 | tf_op jit(solution)/shard_map/reduce_scatter | solution.py:68
  65.3 45.2 %copy-start.1 = (bf16[2,64,256]{2,1,0:T(8,128)(2,1)S(1)}, bf16[2,64,256]{2,1,0:T(8,128)(2,1)}, u32[]{:S(2)}) copy-start(bf16[2,64,256]{2,1,0:T(8,128)(2,1)} %param.17) | copy-start | bytes 196612
Sparse Core Ops, SparseCore 0:
  59.7 47.4 all-gather.1
  110.1 63.6 reduce-scatter.1
